TPU v7x, 256 devices: a whole 4x4x8 slice. The times are simulated.
256 devices in a mesh: seq: 16 (over x, y), grp: 16 (over z, core).
Axes of the slice: x: 4, y: 4, z: 8, core: 2. Of those that a mesh axis runs over, the one named last changes fastest.
Arguments:
- query_rows: bfloat16 [16, 2048, 4096], P('grp', 'seq'), may hold values from -6 to 6
- key_rows: bfloat16 [16, 2048, 1024], P('grp', 'seq'), may hold values from -6 to 6
- value_rows: bfloat16 [16, 2048, 1024], P('grp', 'seq'), may hold values from -27 to 27
- doc_of_block: int32 [16, 16], P('grp'), may hold values from 0 to 3, never falling along the last dimension, each value on 1 to 8 neighbouring positions
- expert_ids: int32 [16, 2048, 2], P('grp', 'seq'), may hold values from 0 to 7, as said below
- gate_weights: float32 [16, 2048, 2], P('grp', 'seq'), may hold values from 0.1 to 0.9
- norm_gain: float32 [4096], replicated, may hold values from 0.1 to 1.9
- w_in: bfloat16 [2, 7168, 4096], P(None, ('seq', 'grp')), may hold values from -0.09375 to 0.09375
- w_down: bfloat16 [7168, 4096], P(('seq', 'grp')), may hold values from -0.0625 to 0.0625
Outputs:
- layer_out: bfloat16 [16, 2048, 4096], P('grp', 'seq')
Inputs may be any that keep to these rules, and one draw needn't show every extreme that they name: `expert_ids`: each token names 2 different experts; in each aligned block of 128 tokens along a sequence (the tokens of one device) at most 40 tokens name expert 0, and in every draw some block has exactly 40 such tokens.
All inputs are finite; a program needn't handle non-finite values.
Results may differ from a plain program's by a relative error of at most 0.014.
Values may be sent and summed in bfloat16 or wider, within the bound.
No kernel may reach another device: no remote copies, remote signals or barrier semaphores. Data moves between devices by JAX's collectives and lax.ppermute only.
A program may use at most 128 MiB of HBM per device.

v0:
```python
import math
import jax
import jax.numpy as jnp
from jax import lax
from jax.sharding import PartitionSpec as P

QH = 32
KVH = 8
HD = 128
BLK = 128
CAP = 40
EPS = 1e-05
NEG = -1e30


def project_in(gathered, piece):
    return jnp.einsum("rd,khd->krh", gathered, piece, preferred_element_type=jnp.float32)


def activate(gate_up):
    return (jax.nn.silu(gate_up[0]) * gate_up[1]).astype(jnp.bfloat16)


def add_down(hidden, piece):
    return jnp.dot(hidden, piece, preferred_element_type=jnp.float32)


def attend(query_all, key_all, value_all, token_doc, per_dev, kv_local):
    seq_length = query_all.shape[1]
    tile_rows = min(512, seq_length)
    tile_count = seq_length // tile_rows
    per_kv = per_dev // kv_local
    inv_root = 1.0 / math.sqrt(HD)
    query_split = query_all[0].reshape(seq_length, kv_local, per_kv, HD)
    key_split = key_all[0].reshape(seq_length, kv_local, HD)
    value_split = value_all[0].reshape(seq_length, kv_local, HD)
    outputs = []
    for q_index in range(tile_count):
        query_tile = query_split[q_index * tile_rows : (q_index + 1) * tile_rows]
        doc_query = token_doc[q_index * tile_rows : (q_index + 1) * tile_rows]
        allowed_row = doc_query[:, None] == token_doc[None, :]
        scores = (
            jnp.einsum("qkgd,tkd->kgqt", query_tile, key_split, preferred_element_type=jnp.float32)
            * inv_root
        )
        scores = jnp.where(allowed_row, scores, NEG)
        highest = jnp.max(scores, axis=3, keepdims=True)
        weights = jnp.exp(scores - highest)
        denom = jnp.sum(weights, axis=3, keepdims=True)
        mixed = jnp.einsum(
            "kgqt,tkd->qkgd",
            weights.astype(jnp.bfloat16),
            value_split,
            preferred_element_type=jnp.float32,
        )
        mixed = mixed / jnp.transpose(denom, (2, 0, 1, 3))
        outputs.append(mixed.reshape(tile_rows, per_dev * HD).astype(jnp.bfloat16))
    return jnp.concatenate(outputs, axis=0)[None]


def shards(
    query_rows,
    key_rows,
    value_rows,
    doc_of_block,
    expert_ids,
    gate_weights,
    norm_gain,
    w_in,
    w_down,
):
    seq_count = lax.axis_size("seq")
    tok_count = query_rows.shape[1]
    per_dev = QH // seq_count
    repeat_count = max(1, 4 // per_dev)
    kv_local = KVH * repeat_count // seq_count
    key_send = jnp.repeat(key_rows.reshape(1, tok_count, KVH, HD), repeat_count, axis=2).reshape(
        1, tok_count, KVH * repeat_count * HD
    )
    value_send = jnp.repeat(
        value_rows.reshape(1, tok_count, KVH, HD), repeat_count, axis=2
    ).reshape(1, tok_count, KVH * repeat_count * HD)
    query_all, key_all, value_all = (
        lax.all_to_all(query_rows, "seq", split_axis=2, concat_axis=1, tiled=True),
        lax.all_to_all(key_send, "seq", split_axis=2, concat_axis=1, tiled=True),
        lax.all_to_all(value_send, "seq", split_axis=2, concat_axis=1, tiled=True),
    )
    token_doc = jnp.repeat(doc_of_block[0], BLK)
    attended = attend(query_all, key_all, value_all, token_doc, per_dev, kv_local)
    attn_tokens = lax.all_to_all(attended, "seq", split_axis=1, concat_axis=2, tiled=True)
    attn_float = attn_tokens[0].astype(jnp.float32)
    spread = jnp.mean(attn_float * attn_float, axis=-1, keepdims=True)
    normed = (attn_float * lax.rsqrt(spread + EPS) * norm_gain).astype(jnp.bfloat16)
    chosen = expert_ids[0] == 0
    routed = jnp.any(chosen, axis=-1)
    gate_share = jnp.sum(jnp.where(chosen, gate_weights[0], 0.0), axis=-1)
    slot_index = jnp.cumsum(routed.astype(jnp.int32)) - 1
    onehot = (slot_index[None, :] == jnp.arange(CAP, dtype=jnp.int32)[:, None]) & routed[None, :]
    dispatched = jnp.dot(
        onehot.astype(jnp.bfloat16), normed, preferred_element_type=jnp.float32
    ).astype(jnp.bfloat16)
    gathered = lax.all_gather(dispatched, "grp", axis=0, tiled=True)
    gate_up = project_in(gathered, lax.all_gather(w_in, "seq", axis=1, tiled=True))
    hidden = activate(gate_up)
    terms = add_down(hidden, lax.all_gather(w_down, "seq", axis=0, tiled=True))
    returned = lax.psum_scatter(
        terms.astype(jnp.bfloat16), "grp", scatter_dimension=0, tiled=True
    ).astype(jnp.float32)
    picked_rows = jnp.take(returned, jnp.clip(slot_index, 0, CAP - 1), axis=0)
    expert_out = jnp.where(routed[:, None], picked_rows, 0.0)
    layer_out = attn_float + gate_share[:, None] * expert_out
    return layer_out.astype(jnp.bfloat16)[None]


def solution(mesh):
    return jax.shard_map(
        shards,
        mesh=mesh,
        in_specs=(
            P("grp", "seq", None),
            P("grp", "seq", None),
            P("grp", "seq", None),
            P("grp", None),
            P("grp", "seq", None),
            P("grp", "seq", None),
            P(),
            P(None, ("seq", "grp"), None),
            P(("seq", "grp"), None),
        ),
        out_specs=P("grp", "seq", None),
        check_vma=False,
    )
```

profile of v0, /device:TPU:2, one launch (start us, length us, event | category | flops | bytes accessed | tf_op | source)
XLA Modules:
  0.0 441.8 jit_solution(3743156761703894871)
XLA Ops:
  7.9 8.1 %copy.145 = bf16[1,128,2048]{1,0,2:T(2,128)(2,1)S(1)} copy(bf16[1,128,2048]{1,2,0:T(8,128)(2,1)S(1)} %bitcast.306) | data formatting | bytes 1048576 | tf_op jit(solution)/shard_map/broadcast_in_dim | solution.py:77
  16.5 11.5 %reduce.20 = bf16[2048,128]{1,0:T(8,128)(2,1)S(1)} reduce(bf16[2048,1,128]{2,1,0:T(2,128)(2,1)S(1)} %bitcast.304, bf16[]{:T(256)} %broadcast.226), dimensions={1}, to_apply=%bitcast.292.reduce_sub_computation | reduce | bytes 1048578
  29.0 7.5 %all-to-all-start = ((bf16[16,2,8192]{2,1,0:T(2,128)(2,1)}), bf16[16,2,8192]{2,1,0:T(2,128)(2,1)S(1)}, u32[]{:S(2)}, u32[]{:S(2)}) async-start(bf16[16,2,8192]{2,1,0:T(2,128)(2,1)} %reshape.333), calls=%async_computation | async-start | bytes 1048576 | tf_op jit(solution)/shard_map/all_to_all | solution.py:85
  36.5 10.8 %all-gather.9.cloned.1.call-start = ((), (), s32[]{:S(2)}) async-start(), calls=%async_computation.8 | async-start | bytes 4456448 | tf_op jit(solution)/shard_map/all_gather | solution.py:105
  48.5 8.1 %copy.144 = bf16[1,128,2048]{1,0,2:T(2,128)(2,1)S(1)} copy(bf16[1,128,2048]{1,2,0:T(8,128)(2,1)S(1)} %bitcast.307) | data formatting | bytes 1048576 | tf_op jit(solution)/shard_map/broadcast_in_dim | solution.py:80
  56.6 11.5 %reduce.19 = bf16[2048,128]{1,0:T(8,128)(2,1)S(1)} reduce(bf16[2048,1,128]{2,1,0:T(2,128)(2,1)S(1)} %bitcast.305, bf16[]{:T(256)} %broadcast.226), dimensions={1}, to_apply=%bitcast.291.reduce_sub_computation | reduce | bytes 1048578
  69.1 7.2 %all-to-all-start.2 = ((bf16[16,2,8192]{2,1,0:T(2,128)(2,1)}), bf16[16,2,8192]{2,1,0:T(2,128)(2,1)}, u32[]{:S(2)}, u32[]{:S(2)}) async-start(bf16[16,2,8192]{2,1,0:T(2,128)(2,1)} %reshape.331), calls=%async_computation.2 | async-start | bytes 1048576 | tf_op jit(solution)/shard_map/all_to_all | solution.py:86
  76.4 2.8 copy.84
  79.2 22.4 %reduce.21 = bf16[4096,128]{1,0:T(8,128)(2,1)S(1)} reduce(bf16[4096,1,128]{2,1,0:T(2,128)(2,1)S(1)} %bitcast.299, bf16[]{:T(256)} %broadcast.226), dimensions={1}, to_apply=%bitcast.272.reduce_sub_computation | reduce | bytes 2097154
  102.9 7.7 %all-to-all-start.1 = ((bf16[16,2,16384]{2,1,0:T(2,128)(2,1)}), bf16[16,2,16384]{2,1,0:T(2,128)(2,1)S(1)}, u32[]{:S(2)}, u32[]{:S(2)}) async-start(bf16[16,2,16384]{2,1,0:T(2,128)(2,1)} %reshape.335), calls=%async_computation.1 | async-start | bytes 2097152 | tf_op jit(solution)/shard_map/all_to_all | solution.py:84
  110.7 3.8 broadcast_compare_fusion.3
  121.5 3.1 all-to-all-done.1
  126.1 3.3 fusion.10
  131.5 2.6 fusion.59
  134.4 2.9 fusion.11
  139.6 2.6 fusion.65
  142.6 2.9 fusion.12
  147.6 3.3 fusion.71
  156.7 2.6 fusion.77
  159.5 11.7 %copy.143 = bf16[1,2048,256]{2,0,1:T(2,128)(2,1)S(1)} copy(bf16[1,2048,256]{2,1,0:T(8,128)(2,1)S(1)} %maximum_bitcast_fusion) | data formatting | bytes 2097152 | tf_op jit(solution)/shard_map/broadcast_in_dim | solution.py:58
  171.3 10.6 %reduce.22 = bf16[2048,256]{1,0:T(8,128)(2,1)S(1)} reduce(bf16[2048,1,256]{2,1,0:T(2,128)(2,1)S(1)} %bitcast.297, bf16[]{:T(256)} %broadcast.226), dimensions={1}, to_apply=%bitcast.290.reduce_sub_computation | reduce | bytes 2097154
  183.0 5.6 %all-to-all-start.3 = ((bf16[16,2,16384]{2,1,0:T(2,128)(2,1)}), bf16[16,2,16384]{2,1,0:T(2,128)(2,1)S(1)}, u32[]{:S(2)}, u32[]{:S(2)}) async-start(bf16[16,2,16384]{2,1,0:T(2,128)(2,1)} %reshape.337), calls=%async_computation.3 | async-start | bytes 2097152 | tf_op jit(solution)/shard_map/all_to_all | solution.py:90
  189.1 13.6 %all-to-all-done.3 = bf16[16,2,16384]{2,1,0:T(2,128)(2,1)S(1)} async-done(((bf16[16,2,16384]{2,1,0:T(2,128)(2,1)}), bf16[16,2,16384]{2,1,0:T(2,128)(2,1)S(1)}, u32[]{:S(2)}, u32[]{:S(2)}) %all-to-all-start.3) | async-done | bytes 1048608 | tf_op jit(solution)/shard_map/all_to_all | solution.py:90
  206.6 15.4 %multiply_reduce_fusion = f32[2048]{0:T(1024)S(1)} fusion(bf16[2048,1,256]{2,1,0:T(2,128)(2,1)S(1)} %reshape.338), kind=kLoop, calls=%fused_computation.44 | loop fusion | flops 1570816 | bytes 1056768 | tf_op jit(solution)/shard_map/reduce_sum | solution.py:92
  224.0 5.1 %reshape.324 = bf16[448,4096]{1,0:T(8,128)(2,1)} reshape(bf16[16,28,4096]{2,1,0:T(8,128)(2,1)} %all-gather.9.cloned.1.call-done) | data formatting | bytes 7340032
  229.1 38.4 %all-gather.5.cloned.1.call-done = bf16[640,4096]{1,0:T(8,128)(2,1)} async-done(((bf16[40,4096]{1,0:T(8,128)(2,1)}), bf16[640,4096]{1,0:T(8,128)(2,1)}) %all-gather.5.cloned.1.call-update) | async-done | bytes 5242896 | tf_op jit(solution)/shard_map/all_gather | solution.py:102
  267.5 72.1 %all-gather.7.cloned.1.call-done = bf16[2,448,4096]{2,0,1:T(2,128)(2,1)} async-done(((bf16[2,28,4096]{2,0,1:T(2,128)(2,1)}), bf16[2,448,4096]{2,0,1:T(2,128)(2,1)}) %all-gather.7.cloned.1.call-update) | async-done | bytes 7340048 | tf_op jit(solution)/shard_map/all_gather | solution.py:103
  339.6 18.5 %fusion.35 = f32[2,640,448]{1,2,0:T(8,128)S(1)} fusion(bf16[2,448,4096]{2,0,1:T(2,128)(2,1)} %all-gather.7.cloned.1.call-done, bf16[640,4096]{1,0:T(8,128)(2,1)} %all-gather.5.cloned.1.call-done), kind=kOutput, calls=%fused_computation.49 | convolution fusion | flops 4697620480 | bytes 14876672 | tf_op jit(solution)/shard_map/rd,khd->krh/dot_general | solution.py:17
  358.2 4.8 %convolution_convert_fusion = bf16[640,4096]{1,0:T(8,128)(2,1)} fusion(bf16[448,4096]{1,0:T(8,128)(2,1)S(1)} %copy-done.4, f32[2,640,448]{1,2,0:T(8,128)S(1)} %fusion.35), kind=kOutput, calls=%fused_computation.23 | convolution fusion | flops 2353152000 | bytes 11206656 | tf_op jit(solution)/shard_map/dot_general | solution.py:25
  363.0 2.6 copy.142
  367.4 60.8 %reduce-scatter.2.cloned.1.call-done = bf16[40,4096]{1,0:T(8,128)(2,1)} async-done(((bf16[640,4096]{1,0:T(8,128)(2,1)}), bf16[40,4096]{1,0:T(8,128)(2,1)}) %reduce-scatter.2.cloned.1.call-update) | async-done | bytes 327696 | tf_op jit(solution)/shard_map/reduce_scatter | solution.py:106
  431.7 3.1 fusion.34
  (100 shorter events, 40.4 us)
Async XLA Ops:
  6.5 69.8 %copy-start.13 = (s32[1,16]{1,0:T(1,128)S(1)}, s32[1,16]{1,0:T(1,128)}, u32[]{:S(2)}) copy-start(s32[1,16]{1,0:T(1,128)} %param.12) | copy-start | bytes 196
  6.5 69.9 %copy-start.6 = (bf16[1,128,4096]{2,1,0:T(8,128)(2,1)S(1)}, bf16[1,128,4096]{2,1,0:T(8,128)(2,1)}, u32[]{:S(2)}) copy-start(bf16[1,128,4096]{2,1,0:T(8,128)(2,1)} %param.9) | copy-start | bytes 3145732
  29.0 40.1 %all-to-all-start = ((bf16[16,2,8192]{2,1,0:T(2,128)(2,1)}), bf16[16,2,8192]{2,1,0:T(2,128)(2,1)S(1)}, u32[]{:S(2)}, u32[]{:S(2)}) async-start(bf16[16,2,8192]{2,1,0:T(2,128)(2,1)} %reshape.333), calls=%async_computation | async-start | bytes 1048576 | tf_op jit(solution)/shard_map/all_to_all | solution.py:85
  36.5 187.5 %all-gather.9.cloned.1.call-start = ((), (), s32[]{:S(2)}) async-start(), calls=%async_computation.8 | async-start | bytes 4456448 | tf_op jit(solution)/shard_map/all_gather | solution.py:105
  69.1 7.2 %copy-start.5 = (bf16[16,2,8192]{2,1,0:T(2,128)(2,1)}, bf16[16,2,8192]{2,1,0:T(2,128)(2,1)S(1)}, u32[]{:S(2)}) copy-start(bf16[16,2,8192]{2,1,0:T(2,128)(2,1)S(1)} %all-to-all-done) | copy-start | bytes 1572868
  69.1 33.8 %all-to-all-start.2 = ((bf16[16,2,8192]{2,1,0:T(2,128)(2,1)}), bf16[16,2,8192]{2,1,0:T(2,128)(2,1)}, u32[]{:S(2)}, u32[]{:S(2)}) async-start(bf16[16,2,8192]{2,1,0:T(2,128)(2,1)} %reshape.331), calls=%async_computation.2 | async-start | bytes 1048576 | tf_op jit(solution)/shard_map/all_to_all | solution.py:86
  102.9 21.7 %all-to-all-start.1 = ((bf16[16,2,16384]{2,1,0:T(2,128)(2,1)}), bf16[16,2,16384]{2,1,0:T(2,128)(2,1)S(1)}, u32[]{:S(2)}, u32[]{:S(2)}) async-start(bf16[16,2,16384]{2,1,0:T(2,128)(2,1)} %reshape.335), calls=%async_computation.1 | async-start | bytes 2097152 | tf_op jit(solution)/shard_map/all_to_all | solution.py:84
  125.8 3.6 copy-start.3
  126.1 5.3 %copy-start.8 = (bf16[2048,128,1]{0,1,2:T(8,128)(2,1)S(1)}, bf16[2048,128,1]{0,1,2:T(8,128)(2,1)}, u32[]{:S(2)}) copy-start(bf16[2048,128,1]{0,1,2:T(8,128)(2,1)} %reshape.326) | copy-start | bytes 1572868
  131.4 3.0 copy-start.2
  134.4 5.1 %copy-start.9 = (bf16[2048,128,1]{0,1,2:T(8,128)(2,1)S(1)}, bf16[2048,128,1]{0,1,2:T(8,128)(2,1)}, u32[]{:S(2)}) copy-start(bf16[2048,128,1]{0,1,2:T(8,128)(2,1)} %reshape.326) | copy-start | bytes 1572868
  139.6 3.0 copy-start.1
  142.6 5.0 %copy-start.10 = (bf16[2048,128,1]{0,1,2:T(8,128)(2,1)S(1)}, bf16[2048,128,1]{0,1,2:T(8,128)(2,1)}, u32[]{:S(2)}) copy-start(bf16[2048,128,1]{0,1,2:T(8,128)(2,1)} %reshape.326) | copy-start | bytes 1572868
  147.5 4.6 %copy-start = (pred[512,2048]{0,1:T(8,128)(4,1)S(1)}, pred[512,2048]{0,1:T(8,128)(4,1)}, u32[]{:S(2)}) copy-start(pred[512,2048]{0,1:T(8,128)(4,1)} %get-tuple-element.14) | copy-start | bytes 3145732
  147.6 4.6 %copy-start.7 = (bf16[1,16,128,128]{3,2,1,0:T(8,128)(2,1)S(1)}, bf16[1,16,128,128]{3,2,1,0:T(8,128)(2,1)}, u32[]{:S(2)}) copy-start(bf16[1,16,128,128]{3,2,1,0:T(8,128)(2,1)} %copy.83) | copy-start | bytes 1572868
  152.2 4.5 %copy-start.11 = (bf16[2048,128,1]{0,1,2:T(8,128)(2,1)S(1)}, bf16[2048,128,1]{0,1,2:T(8,128)(2,1)}, u32[]{:S(2)}) copy-start(bf16[2048,128,1]{0,1,2:T(8,128)(2,1)} %reshape.326) | copy-start | bytes 1572868
  159.3 29.3 %copy-start.14 = (s32[1,128,2]{1,2,0:T(2,128)S(1)}, s32[1,128,2]{1,2,0:T(2,128)}, u32[]{:S(2)}) copy-start(s32[1,128,2]{1,2,0:T(2,128)} %param.13) | copy-start | bytes 3076
  183.0 39.1 %copy-start.12 = (f32[4096]{0:T(1024)S(1)}, f32[4096]{0:T(1024)}, u32[]{:S(2)}) copy-start(f32[4096]{0:T(1024)} %param.15) | copy-start | bytes 49156
  183.0 19.7 %all-to-all-start.3 = ((bf16[16,2,16384]{2,1,0:T(2,128)(2,1)}), bf16[16,2,16384]{2,1,0:T(2,128)(2,1)S(1)}, u32[]{:S(2)}, u32[]{:S(2)}) async-start(bf16[16,2,16384]{2,1,0:T(2,128)(2,1)} %reshape.337), calls=%async_computation.3 | async-start | bytes 2097152 | tf_op jit(solution)/shard_map/all_to_all | solution.py:90
  188.6 78.9 %all-gather.5.cloned.1.call-start = ((), (), s32[]{:S(2)}) async-start(), calls=%async_computation.5 | async-start | bytes 5570560 | tf_op jit(solution)/shard_map/all_gather | solution.py:102
  223.2 116.4 %all-gather.7.cloned.1.call-start = ((), (), s32[]{:S(2)}) async-start(), calls=%async_computation.6 | async-start | bytes 7798784 | tf_op jit(solution)/shard_map/all_gather | solution.py:103
  223.9 204.2 %reduce-scatter.2.cloned.1.call-start = ((), (), s32[]{:S(2)}) async-start(), calls=%async_computation.7 | async-start | bytes 5570560 | tf_op jit(solution)/shard_map/reduce_scatter | solution.py:106
  339.6 18.6 %copy-start.4 = (bf16[448,4096]{1,0:T(8,128)(2,1)S(1)}, bf16[448,4096]{1,0:T(8,128)(2,1)}, u32[]{:S(2)}) copy-start(bf16[448,4096]{1,0:T(8,128)(2,1)} %reshape.324) | copy-start | bytes 11010052
  358.2 4.8 %copy-start.15 = (f32[1,128,2]{1,2,0:T(2,128)S(1)}, f32[1,128,2]{1,2,0:T(2,128)}, u32[]{:S(2)}) copy-start(f32[1,128,2]{1,2,0:T(2,128)} %param.14) | copy-start | bytes 3076
Sparse Core Ops, SparseCore 0:
  47.4 59.1 all-gather.8
  223.3 44.1 all-gather.4
  270.0 69.6 all-gather.6
  363.1 64.9 reduce-scatter.1
where the time goes:
time: 450 us; the launch traced here: 442 us
  waiting for transfers between devices  189 us (42%)
  other arithmetic  88.2 us (20%)
  local copies, waits for them, and re-layouts  64.8 us (14%)
  matrix products  46.9 us (10%)
  starting transfers between devices  38.9 us (9%)
  between operations  14.1 us (3%)
    all_gather x1, waiting for transfers between devices, shards(): lax.all_gather(w_in, 'seq', axis=1, tiled=True)  72.1 us
    reduce_scatter x1, waiting for transfers between devices, shards(): lax.psum_scatter(terms.astype(jnp.bfloat16), 'grp', scatter_dimension=0,...  60.8 us
    unnamed x4, other arithmetic  56 us
    all_gather x1, waiting for transfers between devices, shards(): gathered = lax.all_gather(dispatched, 'grp', axis=0, tiled=True)  38.4 us
    unnamed x47, local copies, waits for them, and re-layouts  21 us
    dot_general x1, matrix products, project_in(): jnp.einsum('rd,khd->krh', gathered, piece, preferred_element_type=jnp.flo...  18.5 us
    reduce_sum x2, other arithmetic, shards(): spread = jnp.mean(attn_float * attn_float, axis=-1, keepdims=True)  15.4 us
    all_to_all x1, waiting for transfers between devices, shards(): lax.all_to_all(attended, 'seq', split_axis=1, concat_axis=2, tiled=True)  13.6 us
  transfers between devices with their start and end apart: 8, of which 5 were waited for; matrix products, arithmetic and copies ran while one was open for 33% of the time, Pallas kernels for 0%

commit v1 on v0

--- a/solution.py
+++ b/solution.py
@@ -87,7 +87,23 @@
     )
     token_doc = jnp.repeat(doc_of_block[0], BLK)
     attended = attend(query_all, key_all, value_all, token_doc, per_dev, kv_local)
-    attn_tokens = lax.all_to_all(attended, "seq", split_axis=1, concat_axis=2, tiled=True)
+    arr_out = jax.lax.axis_size("seq")
+    top, small = (arr_out, jax.lax.axis_index("seq"))
+    carry = attended.shape[1] // top
+    mat_out = list(attended.shape)
+    mat_out[1] = carry
+    o_now = mat_out[2]
+    mat_out[2] = o_now * top
+    attn_tokens = jnp.zeros(mat_out, attended.dtype)
+    dev = 0
+    while dev < top:
+        t_next = lax.dynamic_slice_in_dim(attended, (small ^ dev) * carry, carry, axis=1)
+        if dev:
+            t_next = jax.lax.ppermute(t_next, "seq", [(tick, tick ^ dev) for tick in range(top)])
+        attn_tokens = lax.dynamic_update_slice_in_dim(
+            attn_tokens, t_next, (small ^ dev) * o_now, axis=2
+        )
+        dev += 1
     attn_float = attn_tokens[0].astype(jnp.float32)
     spread = jnp.mean(attn_float * attn_float, axis=-1, keepdims=True)
     normed = (attn_float * lax.rsqrt(spread + EPS) * norm_gain).astype(jnp.bfloat16)

time: 450 us -> 415 us (0.922)
  other arithmetic: 88.2 us -> 62.2 us
  local copies, waits for them, and re-layouts: 64.8 us -> 44.1 us
  starting transfers between devices: 38.9 us -> 52.5 us
    ppermute x0 -> x15, starting transfers between devices: none -> 29.8 us  [shards(): jax.lax.ppermute(t_next, 'seq', [(tick, tick ^ dev) for tick in range(top)])]
    reduce_sum x2 -> x1, other arithmetic: 15.4 us -> 0.28 us  [shards(): spread = jnp.mean(attn_float * attn_float, axis=-1, keepdims=True)]
    all_to_all x1 -> x0, waiting for transfers between devices: 13.6 us -> none  [shards(): lax.all_to_all(attended, 'seq', split_axis=1, concat_axis=2, tiled=True)]
    broadcast_in_dim x1 -> x0, local copies, waits for them, and re-layouts: 11.7 us -> none  [attend(): return jnp.concatenate(outputs, axis=0)[None]]
    unnamed x4 -> x3, other arithmetic: 56 us -> 45.2 us
    all_gather x1, starting transfers between devices: 10.8 us -> 0.25 us  [shards(): terms = add_down(hidden, lax.all_gather(w_down, 'seq', axis=0, tiled=True))]
    all_to_all x1 -> x0, starting transfers between devices: 5.61 us -> none  [shards(): lax.all_to_all(attended, 'seq', split_axis=1, concat_axis=2, tiled=True)]
    convert_element_type x3 -> x0, local copies, waits for them, and re-layouts: 5.55 us -> none  [shards(): attn_float = attn_tokens[0].astype(jnp.float32)]
  transfers between devices with their start and end apart: 8 -> 22, of which waited for: 5 -> 6; matrix products, arithmetic and copies ran while one was open for 33% -> 25% of each run, Pallas kernels for 0% -> 0%
where the time goes in v1:
time: 415 us; the launch traced here: 407 us
  waiting for transfers between devices  187 us (45%)
  other arithmetic  62.2 us (15%)
  starting transfers between devices  52.5 us (13%)
  matrix products  46.3 us (11%)
  local copies, waits for them, and re-layouts  44.1 us (11%)
  between operations  14.6 us (4%)
    all_gather x1, waiting for transfers between devices, shards(): lax.all_gather(w_in, 'seq', axis=1, tiled=True)  72.1 us
    reduce_scatter x1, waiting for transfers between devices, shards(): lax.psum_scatter(terms.astype(jnp.bfloat16), 'grp', scatter_dimension=0,...  65.1 us
    unnamed x3, other arithmetic  45.2 us
    all_gather x1, waiting for transfers between devices, shards(): gathered = lax.all_gather(dispatched, 'grp', axis=0, tiled=True)  42 us
    ppermute x15, starting transfers between devices, shards(): jax.lax.ppermute(t_next, 'seq', [(tick, tick ^ dev) for tick in range(top)])  29.8 us
    dot_general x1, matrix products, project_in(): jnp.einsum('rd,khd->krh', gathered, piece, preferred_element_type=jnp.flo...  18.5 us
    unnamed x44, local copies, waits for them, and re-layouts  17.2 us
    dot_general x4, matrix products, attend(): jnp.einsum('kgqt,tkd->qkgd', weights.astype(jnp.bfloat16), value_split, p...  11.8 us
  transfers between devices with their start and end apart: 22, of which 6 were waited for; matrix products, arithmetic and copies ran while one was open for 25% of the time, Pallas kernels for 0%

profile of v1, /device:TPU:2, one launch (start us, length us, event | category | flops | bytes accessed | tf_op | source)
XLA Modules:
  0.0 407.2 jit_solution(9630025417798686421)
XLA Ops:
  7.9 8.1 %copy.116 = bf16[1,128,2048]{1,0,2:T(2,128)(2,1)S(1)} copy(bf16[1,128,2048]{1,2,0:T(8,128)(2,1)S(1)} %bitcast.333) | data formatting | bytes 1048576 | tf_op jit(solution)/shard_map/broadcast_in_dim | solution.py:77
  16.5 11.4 %reduce.15 = bf16[2048,128]{1,0:T(8,128)(2,1)S(1)} reduce(bf16[2048,1,128]{2,1,0:T(2,128)(2,1)S(1)} %bitcast.331, bf16[]{:T(256)} %broadcast.171), dimensions={1}, to_apply=%bitcast.325.reduce_sub_computation | reduce | bytes 1048578
  28.9 7.5 %all-to-all-start = ((bf16[16,2,8192]{2,1,0:T(2,128)(2,1)}), bf16[16,2,8192]{2,1,0:T(2,128)(2,1)S(1)}, u32[]{:S(2)}, u32[]{:S(2)}) async-start(bf16[16,2,8192]{2,1,0:T(2,128)(2,1)} %reshape.286), calls=%async_computation | async-start | bytes 1048576 | tf_op jit(solution)/shard_map/all_to_all | solution.py:85
  38.3 8.1 %copy.115 = bf16[1,128,2048]{1,0,2:T(2,128)(2,1)S(1)} copy(bf16[1,128,2048]{1,2,0:T(8,128)(2,1)S(1)} %bitcast.334) | data formatting | bytes 1048576 | tf_op jit(solution)/shard_map/broadcast_in_dim | solution.py:80
  46.5 11.4 %reduce.14 = bf16[2048,128]{1,0:T(8,128)(2,1)S(1)} reduce(bf16[2048,1,128]{2,1,0:T(2,128)(2,1)S(1)} %bitcast.332, bf16[]{:T(256)} %broadcast.171), dimensions={1}, to_apply=%bitcast.324.reduce_sub_computation | reduce | bytes 1048578
  58.9 7.2 %all-to-all-start.2 = ((bf16[16,2,8192]{2,1,0:T(2,128)(2,1)}), bf16[16,2,8192]{2,1,0:T(2,128)(2,1)}, u32[]{:S(2)}, u32[]{:S(2)}) async-start(bf16[16,2,8192]{2,1,0:T(2,128)(2,1)} %reshape.284), calls=%async_computation.2 | async-start | bytes 1048576 | tf_op jit(solution)/shard_map/all_to_all | solution.py:86
  66.3 2.8 copy.62
  69.2 22.3 %reduce.16 = bf16[4096,128]{1,0:T(8,128)(2,1)S(1)} reduce(bf16[4096,1,128]{2,1,0:T(2,128)(2,1)S(1)} %bitcast.327, bf16[]{:T(256)} %broadcast.171), dimensions={1}, to_apply=%bitcast.311.reduce_sub_computation | reduce | bytes 2097154
  93.2 7.2 %all-to-all-start.1 = ((bf16[16,2,16384]{2,1,0:T(2,128)(2,1)}), bf16[16,2,16384]{2,1,0:T(2,128)(2,1)S(1)}, u32[]{:S(2)}, u32[]{:S(2)}) async-start(bf16[16,2,16384]{2,1,0:T(2,128)(2,1)} %reshape.288), calls=%async_computation.1 | async-start | bytes 2097152 | tf_op jit(solution)/shard_map/all_to_all | solution.py:84
  101.0 3.8 broadcast_compare_fusion.3
  111.8 2.8 all-to-all-done.1
  116.3 3.3 fusion.10
  121.6 2.6 fusion.61
  124.3 2.2 fusion.11
  128.7 3.3 fusion.67
  136.5 3.3 fusion.73
  145.9 2.6 fusion.79
  149.8 2.3 collective-permute-start.1
  156.0 3.1 collective-permute-start.5
  163.7 4.5 %collective-permute-start.9 = (bf16[1,128,256]{2,1,0:T(8,128)(2,1)S(1)}, bf16[1,128,256]{2,1,0:T(8,128)(2,1)S(1)}, u32[]{:S(2)}, u32[]{:S(2)}) collective-permute-start(bf16[1,128,256]{2,1,0:T(8,128)(2,1)S(1)} %get-tuple-element.12), channel_id=1, source_target_pairs={{0,160},{16,176},{32,128},{48,144},{64,224},{80,240},{96,192},{112... | collective-permute-start | bytes 196616 | tf_op jit(solution)/shard_map/ppermute | solution.py:102
  168.2 3.5 collective-permute-start.10
  173.0 4.0 collective-permute-start.13
  176.9 2.2 collective-permute-start.14
  179.8 3.6 collective-permute-done.14
  185.8 5.0 %reshape.277 = bf16[448,4096]{1,0:T(8,128)(2,1)} reshape(bf16[16,28,4096]{2,1,0:T(8,128)(2,1)} %all-gather.9.cloned.1.call-done) | data formatting | bytes 7340032
  190.8 42.0 %all-gather.5.cloned.1.call-done = bf16[640,4096]{1,0:T(8,128)(2,1)} async-done(((bf16[40,4096]{1,0:T(8,128)(2,1)}), bf16[640,4096]{1,0:T(8,128)(2,1)}) %all-gather.5.cloned.1.call-update) | async-done | bytes 5242896 | tf_op jit(solution)/shard_map/all_gather | solution.py:118
  232.8 72.1 %all-gather.7.cloned.1.call-done = bf16[2,448,4096]{2,0,1:T(2,128)(2,1)} async-done(((bf16[2,28,4096]{2,0,1:T(2,128)(2,1)}), bf16[2,448,4096]{2,0,1:T(2,128)(2,1)}) %all-gather.7.cloned.1.call-update) | async-done | bytes 7340048 | tf_op jit(solution)/shard_map/all_gather | solution.py:119
  304.9 18.5 %fusion.35 = f32[2,640,448]{1,2,0:T(8,128)S(1)} fusion(bf16[2,448,4096]{2,0,1:T(2,128)(2,1)} %all-gather.7.cloned.1.call-done, bf16[640,4096]{1,0:T(8,128)(2,1)} %all-gather.5.cloned.1.call-done), kind=kOutput, calls=%fused_computation.49 | convolution fusion | flops 4697620480 | bytes 14876672 | tf_op jit(solution)/shard_map/rd,khd->krh/dot_general | solution.py:17
  323.5 4.8 %convolution_convert_fusion = bf16[640,4096]{1,0:T(8,128)(2,1)} fusion(bf16[448,4096]{1,0:T(8,128)(2,1)S(1)} %copy-done.4, f32[2,640,448]{1,2,0:T(8,128)S(1)} %fusion.35), kind=kOutput, calls=%fused_computation.23 | convolution fusion | flops 2353152000 | bytes 11206656 | tf_op jit(solution)/shard_map/dot_general | solution.py:25
  328.4 65.1 %reduce-scatter.2.cloned.1.call-done = bf16[40,4096]{1,0:T(8,128)(2,1)} async-done(((bf16[640,4096]{1,0:T(8,128)(2,1)}), bf16[40,4096]{1,0:T(8,128)(2,1)}) %reduce-scatter.2.cloned.1.call-update) | async-done | bytes 327696 | tf_op jit(solution)/shard_map/reduce_scatter | solution.py:122
  394.5 2.6 gather_fusion
  397.1 3.1 fusion.54
  (136 shorter events, 46.0 us)
Async XLA Ops:
  6.5 52.3 %copy-start.13 = (s32[1,128,2]{1,2,0:T(2,128)S(1)}, s32[1,128,2]{1,2,0:T(2,128)}, u32[]{:S(2)}) copy-start(s32[1,128,2]{1,2,0:T(2,128)} %param.13) | copy-start | bytes 3076
  6.5 52.3 %copy-start.12 = (s32[1,16]{1,0:T(1,128)S(1)}, s32[1,16]{1,0:T(1,128)}, u32[]{:S(2)}) copy-start(s32[1,16]{1,0:T(1,128)} %param.12) | copy-start | bytes 196
  6.5 59.8 %copy-start.6 = (bf16[1,128,4096]{2,1,0:T(8,128)(2,1)S(1)}, bf16[1,128,4096]{2,1,0:T(8,128)(2,1)}, u32[]{:S(2)}) copy-start(bf16[1,128,4096]{2,1,0:T(8,128)(2,1)} %param.9) | copy-start | bytes 3145732
  28.9 30.1 %all-to-all-start = ((bf16[16,2,8192]{2,1,0:T(2,128)(2,1)}), bf16[16,2,8192]{2,1,0:T(2,128)(2,1)S(1)}, u32[]{:S(2)}, u32[]{:S(2)}) async-start(bf16[16,2,8192]{2,1,0:T(2,128)(2,1)} %reshape.286), calls=%async_computation | async-start | bytes 1048576 | tf_op jit(solution)/shard_map/all_to_all | solution.py:85
  36.4 149.4 %all-gather.9.cloned.1.call-start = ((), (), s32[]{:S(2)}) async-start(), calls=%async_computation.7 | async-start | bytes 4456448 | tf_op jit(solution)/shard_map/all_gather | solution.py:121
  58.9 7.4 %copy-start.5 = (bf16[16,2,8192]{2,1,0:T(2,128)(2,1)}, bf16[16,2,8192]{2,1,0:T(2,128)(2,1)S(1)}, u32[]{:S(2)}) copy-start(bf16[16,2,8192]{2,1,0:T(2,128)(2,1)S(1)} %all-to-all-done) | copy-start | bytes 1572868
  58.9 34.3 %all-to-all-start.2 = ((bf16[16,2,8192]{2,1,0:T(2,128)(2,1)}), bf16[16,2,8192]{2,1,0:T(2,128)(2,1)}, u32[]{:S(2)}, u32[]{:S(2)}) async-start(bf16[16,2,8192]{2,1,0:T(2,128)(2,1)} %reshape.284), calls=%async_computation.2 | async-start | bytes 1048576 | tf_op jit(solution)/shard_map/all_to_all | solution.py:86
  93.2 21.4 %all-to-all-start.1 = ((bf16[16,2,16384]{2,1,0:T(2,128)(2,1)}), bf16[16,2,16384]{2,1,0:T(2,128)(2,1)S(1)}, u32[]{:S(2)}, u32[]{:S(2)}) async-start(bf16[16,2,16384]{2,1,0:T(2,128)(2,1)} %reshape.288), calls=%async_computation.1 | async-start | bytes 2097152 | tf_op jit(solution)/shard_map/all_to_all | solution.py:84
  100.4 132.4 %all-gather.5.cloned.1.call-start = ((), (), s32[]{:S(2)}) async-start(), calls=%async_computation.4 | async-start | bytes 5570560 | tf_op jit(solution)/shard_map/all_gather | solution.py:118
  116.3 5.3 %copy-start.8 = (bf16[2048,128,1]{0,1,2:T(8,128)(2,1)S(1)}, bf16[2048,128,1]{0,1,2:T(8,128)(2,1)}, u32[]{:S(2)}) copy-start(bf16[2048,128,1]{0,1,2:T(8,128)(2,1)} %reshape.279) | copy-start | bytes 1572868
  136.5 4.9 %copy-start = (pred[512,2048]{0,1:T(8,128)(4,1)S(1)}, pred[512,2048]{0,1:T(8,128)(4,1)}, u32[]{:S(2)}) copy-start(pred[512,2048]{0,1:T(8,128)(4,1)} %get-tuple-element.30) | copy-start | bytes 3145732
  141.4 4.4 %copy-start.10 = (bf16[2048,128,1]{0,1,2:T(8,128)(2,1)S(1)}, bf16[2048,128,1]{0,1,2:T(8,128)(2,1)}, u32[]{:S(2)}) copy-start(bf16[2048,128,1]{0,1,2:T(8,128)(2,1)} %reshape.279) | copy-start | bytes 1572868
  148.5 35.2 %copy-start.15 = (f32[4096]{0:T(1024)S(1)}, f32[4096]{0:T(1024)}, u32[]{:S(2)}) copy-start(f32[4096]{0:T(1024)} %param.15) | copy-start | bytes 49156
  149.0 7.0 %collective-permute-start = (bf16[1,128,256]{2,1,0:T(8,128)(2,1)S(1)}, bf16[1,128,256]{2,1,0:T(8,128)(2,1)S(1)}, u32[]{:S(2)}, u32[]{:S(2)}) collective-permute-start(bf16[1,128,256]{2,1,0:T(8,128)(2,1)S(1)} %get-tuple-element.21), channel_id=1, source_target_pairs={{0,16},{16,0},{32,48},{48,32},{64,80},{80,64},{96,112},{112,96},{1... | collective-permute-start | bytes 196616 | tf_op jit(solution)/shard_map/ppermute | solution.py:102
  149.8 9.3 %collective-permute-start.1 = (bf16[1,128,256]{2,1,0:T(8,128)(2,1)S(1)}, bf16[1,128,256]{2,1,0:T(8,128)(2,1)S(1)}, u32[]{:S(2)}, u32[]{:S(2)}) collective-permute-start(bf16[1,128,256]{2,1,0:T(8,128)(2,1)S(1)} %get-tuple-element.20), channel_id=1, source_target_pairs={{0,32},{16,48},{32,0},{48,16},{64,96},{80,112},{96,64},{112,80},{1... | collective-permute-start | bytes 196616 | tf_op jit(solution)/shard_map/ppermute | solution.py:102
  152.1 9.1 %collective-permute-start.2 = (bf16[1,128,256]{2,1,0:T(8,128)(2,1)S(1)}, bf16[1,128,256]{2,1,0:T(8,128)(2,1)S(1)}, u32[]{:S(2)}, u32[]{:S(2)}) collective-permute-start(bf16[1,128,256]{2,1,0:T(8,128)(2,1)S(1)} %get-tuple-element.19), channel_id=1, source_target_pairs={{0,48},{16,32},{32,16},{48,0},{64,112},{80,96},{96,80},{112,64},{1... | collective-permute-start | bytes 196616 | tf_op jit(solution)/shard_map/ppermute | solution.py:102
  154.0 9.4 %collective-permute-start.3 = (bf16[1,128,256]{2,1,0:T(8,128)(2,1)S(1)}, bf16[1,128,256]{2,1,0:T(8,128)(2,1)S(1)}, u32[]{:S(2)}, u32[]{:S(2)}) collective-permute-start(bf16[1,128,256]{2,1,0:T(8,128)(2,1)S(1)} %get-tuple-element.18), channel_id=1, source_target_pairs={{0,64},{16,80},{32,96},{48,112},{64,0},{80,16},{96,32},{112,48},{1... | collective-permute-start | bytes 196616 | tf_op jit(solution)/shard_map/ppermute | solution.py:102
  156.0 7.7 %collective-permute-start.4 = (bf16[1,128,256]{2,1,0:T(8,128)(2,1)S(1)}, bf16[1,128,256]{2,1,0:T(8,128)(2,1)S(1)}, u32[]{:S(2)}, u32[]{:S(2)}) collective-permute-start(bf16[1,128,256]{2,1,0:T(8,128)(2,1)S(1)} %get-tuple-element.17), channel_id=1, source_target_pairs={{0,80},{16,64},{32,112},{48,96},{64,16},{80,0},{96,48},{112,32},{1... | collective-permute-start | bytes 196616 | tf_op jit(solution)/shard_map/ppermute | solution.py:102
  156.0 12.2 %collective-permute-start.5 = (bf16[1,128,256]{2,1,0:T(8,128)(2,1)S(1)}, bf16[1,128,256]{2,1,0:T(8,128)(2,1)S(1)}, u32[]{:S(2)}, u32[]{:S(2)}) collective-permute-start(bf16[1,128,256]{2,1,0:T(8,128)(2,1)S(1)} %get-tuple-element.16), channel_id=1, source_target_pairs={{0,96},{16,112},{32,64},{48,80},{64,32},{80,48},{96,0},{112,16},{1... | collective-permute-start | bytes 196616 | tf_op jit(solution)/shard_map/ppermute | solution.py:102
  159.1 12.6 %collective-permute-start.6 = (bf16[1,128,256]{2,1,0:T(8,128)(2,1)S(1)}, bf16[1,128,256]{2,1,0:T(8,128)(2,1)S(1)}, u32[]{:S(2)}, u32[]{:S(2)}) collective-permute-start(bf16[1,128,256]{2,1,0:T(8,128)(2,1)S(1)} %get-tuple-element.15), channel_id=1, source_target_pairs={{0,112},{16,96},{32,80},{48,64},{64,48},{80,32},{96,16},{112,0},{1... | collective-permute-start | bytes 196616 | tf_op jit(solution)/shard_map/ppermute | solution.py:102
  161.2 11.6 %collective-permute-start.7 = (bf16[1,128,256]{2,1,0:T(8,128)(2,1)S(1)}, bf16[1,128,256]{2,1,0:T(8,128)(2,1)S(1)}, u32[]{:S(2)}, u32[]{:S(2)}) collective-permute-start(bf16[1,128,256]{2,1,0:T(8,128)(2,1)S(1)} %get-tuple-element.14), channel_id=1, source_target_pairs={{0,128},{16,144},{32,160},{48,176},{64,192},{80,208},{96,224},{112... | collective-permute-start | bytes 196616 | tf_op jit(solution)/shard_map/ppermute | solution.py:102
  163.4 9.6 %collective-permute-start.8 = (bf16[1,128,256]{2,1,0:T(8,128)(2,1)S(1)}, bf16[1,128,256]{2,1,0:T(8,128)(2,1)S(1)}, u32[]{:S(2)}, u32[]{:S(2)}) collective-permute-start(bf16[1,128,256]{2,1,0:T(8,128)(2,1)S(1)} %get-tuple-element.13), channel_id=1, source_target_pairs={{0,144},{16,128},{32,176},{48,160},{64,208},{80,192},{96,240},{112... | collective-permute-start | bytes 196616 | tf_op jit(solution)/shard_map/ppermute | solution.py:102
  163.7 13.3 %collective-permute-start.9 = (bf16[1,128,256]{2,1,0:T(8,128)(2,1)S(1)}, bf16[1,128,256]{2,1,0:T(8,128)(2,1)S(1)}, u32[]{:S(2)}, u32[]{:S(2)}) collective-permute-start(bf16[1,128,256]{2,1,0:T(8,128)(2,1)S(1)} %get-tuple-element.12), channel_id=1, source_target_pairs={{0,160},{16,176},{32,128},{48,144},{64,224},{80,240},{96,192},{112... | collective-permute-start | bytes 196616 | tf_op jit(solution)/shard_map/ppermute | solution.py:102
  168.2 11.0 %collective-permute-start.10 = (bf16[1,128,256]{2,1,0:T(8,128)(2,1)S(1)}, bf16[1,128,256]{2,1,0:T(8,128)(2,1)S(1)}, u32[]{:S(2)}, u32[]{:S(2)}) collective-permute-start(bf16[1,128,256]{2,1,0:T(8,128)(2,1)S(1)} %get-tuple-element.11), channel_id=1, source_target_pairs={{0,176},{16,160},{32,144},{48,128},{64,240},{80,224},{96,208},{112... | collective-permute-start | bytes 196616 | tf_op jit(solution)/shard_map/ppermute | solution.py:102
  171.7 7.5 %collective-permute-start.11 = (bf16[1,128,256]{2,1,0:T(8,128)(2,1)S(1)}, bf16[1,128,256]{2,1,0:T(8,128)(2,1)S(1)}, u32[]{:S(2)}, u32[]{:S(2)}) collective-permute-start(bf16[1,128,256]{2,1,0:T(8,128)(2,1)S(1)} %get-tuple-element.10), channel_id=1, source_target_pairs={{0,192},{16,208},{32,224},{48,240},{64,128},{80,144},{96,160},{112... | collective-permute-start | bytes 196616 | tf_op jit(solution)/shard_map/ppermute | solution.py:102
  172.8 6.4 %collective-permute-start.12 = (bf16[1,128,256]{2,1,0:T(8,128)(2,1)S(1)}, bf16[1,128,256]{2,1,0:T(8,128)(2,1)S(1)}, u32[]{:S(2)}, u32[]{:S(2)}) collective-permute-start(bf16[1,128,256]{2,1,0:T(8,128)(2,1)S(1)} %get-tuple-element.9), channel_id=1, source_target_pairs={{0,208},{16,192},{32,240},{48,224},{64,144},{80,128},{96,176},{112... | collective-permute-start | bytes 196616 | tf_op jit(solution)/shard_map/ppermute | solution.py:102
  173.0 6.8 %collective-permute-start.13 = (bf16[1,128,256]{2,1,0:T(8,128)(2,1)S(1)}, bf16[1,128,256]{2,1,0:T(8,128)(2,1)S(1)}, u32[]{:S(2)}, u32[]{:S(2)}) collective-permute-start(bf16[1,128,256]{2,1,0:T(8,128)(2,1)S(1)} %get-tuple-element.8), channel_id=1, source_target_pairs={{0,224},{16,240},{32,192},{48,208},{64,160},{80,176},{96,128},{112... | collective-permute-start | bytes 196616 | tf_op jit(solution)/shard_map/ppermute | solution.py:102
  176.9 6.5 %collective-permute-start.14 = (bf16[1,128,256]{2,1,0:T(8,128)(2,1)S(1)}, bf16[1,128,256]{2,1,0:T(8,128)(2,1)S(1)}, u32[]{:S(2)}, u32[]{:S(2)}) collective-permute-start(bf16[1,128,256]{2,1,0:T(8,128)(2,1)S(1)} %get-tuple-element.7), channel_id=1, source_target_pairs={{0,240},{16,224},{32,208},{48,192},{64,176},{80,160},{96,144},{112... | collective-permute-start | bytes 196616 | tf_op jit(solution)/shard_map/ppermute | solution.py:102
  185.0 120.0 %all-gather.7.cloned.1.call-start = ((), (), s32[]{:S(2)}) async-start(), calls=%async_computation.5 | async-start | bytes 7798784 | tf_op jit(solution)/shard_map/all_gather | solution.py:119
  185.7 207.8 %reduce-scatter.2.cloned.1.call-start = ((), (), s32[]{:S(2)}) async-start(), calls=%async_computation.6 | async-start | bytes 5570560 | tf_op jit(solution)/shard_map/reduce_scatter | solution.py:122
  304.9 18.6 %copy-start.4 = (bf16[448,4096]{1,0:T(8,128)(2,1)S(1)}, bf16[448,4096]{1,0:T(8,128)(2,1)}, u32[]{:S(2)}) copy-start(bf16[448,4096]{1,0:T(8,128)(2,1)} %reshape.277) | copy-start | bytes 11010052
  323.5 4.8 %copy-start.14 = (f32[1,128,2]{1,2,0:T(2,128)S(1)}, f32[1,128,2]{1,2,0:T(2,128)}, u32[]{:S(2)}) copy-start(f32[1,128,2]{1,2,0:T(2,128)} %param.14) | copy-start | bytes 3076
  (6 other events, 20.4 us)
Sparse Core Ops, SparseCore 0:
  39.6 59.1 all-gather.8
  185.1 47.6 all-gather.4
  235.3 69.6 all-gather.6
  328.5 64.9 reduce-scatter.1
